TPU v7x, 256 devices: a whole 4x4x8 slice. The times are simulated.
256 devices in a mesh: gx: 16 (over z, core), gy: 16 (over x, y).
Axes of the slice: x: 4, y: 4, z: 8, core: 2. Of those that a mesh axis runs over, the one named last changes fastest.
Arguments:
- state: bfloat16 [2, 256, 768, 2048], P(None, None, 'gx', 'gy'), as said below
Outputs:
- modes: bfloat16 [255, 2, 768, 2048], P(None, None, 'gx', 'gy')
- reduced: float32 [255, 255], replicated
Inputs may be any that keep to these rules, and one draw needn't show every extreme that they name: `state`: both fields are positive.
All inputs are finite; a program needn't handle non-finite values.
Results may differ from a plain program's by a relative error of at most 0.0077.
Values may be sent and summed in bfloat16 or wider, within the bound.
No kernel may reach another device: no remote copies, remote signals or barrier semaphores. Data moves between devices by JAX's collectives and lax.ppermute only.
A program may use at most 128 MiB of HBM per device.

v0:
```python
import jax
import jax.numpy as jnp
from jax import lax
from jax.sharding import PartitionSpec as P


def padded_2(cells, sides, width):
    for axis, dim in sides:
        count = lax.axis_size(axis)
        ends = count - 1
        head = lax.slice_in_dim(cells, 0, width, axis=dim)
        tail = lax.slice_in_dim(cells, cells.shape[dim] - width, cells.shape[dim], axis=dim)
        cells = jnp.concatenate(
            [
                lax.ppermute(tail, axis, [(i, (i + 1) % count) for i in range(ends)]),
                cells,
                lax.ppermute(head, axis, [((i + 1) % count, i) for i in range(ends)]),
            ],
            axis=dim,
        )
    return cells


def tri_solve(lower, right):
    return lax.linalg.triangular_solve(lower, right, left_side=True, lower=True)


def gradients(padded):
    grad_x = (
        padded[:, :-4, 2:-2]
        - 8.0 * padded[:, 1:-3, 2:-2]
        + 8.0 * padded[:, 3:-1, 2:-2]
        - padded[:, 4:, 2:-2]
    ) / 12.0
    grad_y = (
        padded[:, 2:-2, :-4]
        - 8.0 * padded[:, 2:-2, 1:-3]
        + 8.0 * padded[:, 2:-2, 3:-1]
        - padded[:, 2:-2, 4:]
    ) / 12.0
    return jnp.stack([grad_x, grad_y], axis=1).astype(jnp.bfloat16)


def shards(state):
    snaps = state.shape[1]
    rows_x = state.shape[2]
    rows_y = state.shape[3]
    total_rows = 2 * rows_x * rows_y * lax.axis_size("gx") * lax.axis_size("gy")
    temp = 0.4 * state[1].astype(jnp.float32) / state[0].astype(jnp.float32)
    padded = padded_2(temp, (("gx", 1), ("gy", 2)), 2)
    features = gradients(padded)
    snap = features.reshape(snaps, 2 * rows_x * rows_y)
    local_gram = (
        lax.dot_general(snap, snap, (((1,), (1,)), ((), ())), preferred_element_type=jnp.float32)
        / total_rows
    )
    gram = lax.psum(local_gram, ("gx", "gy"))
    lower = jnp.linalg.cholesky(gram[: snaps - 1, : snaps - 1])
    cross = gram[: snaps - 1, 1:]
    half = tri_solve(lower, cross)
    reduced = tri_solve(lower, half.T).T
    inverse = tri_solve(lower, jnp.eye(snaps - 1, dtype=jnp.float32)).astype(jnp.bfloat16)
    modes = jnp.dot(inverse, snap[1:], preferred_element_type=jnp.float32).astype(jnp.bfloat16)
    return (modes.reshape(snaps - 1, 2, rows_x, rows_y), reduced)


def solution(mesh):
    placed = (P(None, None, "gx", "gy"),)
    return jax.shard_map(
        shards,
        mesh=mesh,
        in_specs=placed,
        out_specs=(P(None, None, "gx", "gy"), P()),
        check_vma=False,
    )
```

profile of v0, /device:TPU:2, one launch (start us, length us, event | category | flops | bytes accessed | tf_op | source)
XLA Modules:
  0.0 435.9 jit_solution(15575594914575890213)
XLA Ops:
  7.2 3.9 fusion.44
  12.5 1.8 collective-permute-start
  16.3 3.1 collective-permute-done.1
  20.1 3.6 pad_maximum_fusion.1
  23.7 11.6 %fusion.42 = (f32[256,52,2]{2,0,1:T(8,128)}, f32[256,52,2]{2,0,1:T(8,128)}) fusion(f32[256,52,128]{2,0,1:T(8,128)} %pad_maximum_fusion.1), kind=kLoop, calls=%fused_computation.88 | loop fusion | bytes 425984 | tf_op jit(solution)/shard_map/slice | solution.py:12
  35.4 4.7 %copy.16 = f32[256,52,2]{0,2,1:T(2,128)S(1)} copy(f32[256,52,2]{2,0,1:T(8,128)} %get-tuple-element.41) | data formatting | bytes 212992 | tf_op jit(solution)/shard_map/slice | solution.py:12
  40.1 3.5 collective-permute-start.2
  43.6 5.3 %copy.18 = f32[256,52,2]{0,2,1:T(2,128)} copy(f32[256,52,2]{2,0,1:T(8,128)} %get-tuple-element.42) | data formatting | bytes 212992 | tf_op jit(solution)/shard_map/slice | solution.py:11
  48.9 4.6 %collective-permute-start.3 = (f32[256,52,2]{0,2,1:T(2,128)}, f32[256,52,2]{0,2,1:T(2,128)}, u32[]{:S(2)}, u32[]{:S(2)}) collective-permute-start(f32[256,52,2]{0,2,1:T(2,128)} %copy.18), channel_id=1, source_target_pairs={{1,0},{2,1},{3,2},{4,3},{5,4},{6,5},{7,6},{8,7},{9,8},{10,9},{11,1... | collective-permute-start | bytes 319496 | tf_op jit(solution)/shard_map/ppermute | solution.py:17
  53.5 11.1 %fusion.17 = bf16[256,1,48,128]{3,0,2,1:T(8,128)(2,1)S(1)} fusion(f32[256,2,128]{2,0,1:T(8,128)} %copy-done.2, f32[256,48,128]{2,0,1:T(8,128)} %copy-done, f32[256,2,128]{2,0,1:T(8,128)S(1)} %collective-permute-done), kind=kLoop, calls=%fused_computation.36 | loop fusion | flops 17301504 | bytes 9961472 | tf_op jit(solution)/shard_map/stack | solution.py:41
  64.6 5.0 %copy.17 = f32[256,52,2]{2,0,1:T(8,128)} copy(f32[256,52,2]{0,2,1:T(2,128)} %collective-permute-done.2) | data formatting | bytes 212992 | tf_op jit(solution)/shard_map/ppermute | solution.py:15
  69.6 5.1 %copy.19 = f32[256,52,2]{2,0,1:T(8,128)} copy(f32[256,52,2]{0,2,1:T(2,128)} %collective-permute-done.3) | data formatting | bytes 212992 | tf_op jit(solution)/shard_map/ppermute | solution.py:17
  74.7 21.0 %fusion.18 = bf16[256,1,48,128]{3,0,2,1:T(8,128)(2,1)S(1)} fusion(f32[256,52,2]{2,0,1:T(8,128)} %copy.19, f32[256,2,128]{2,0,1:T(8,128)} %copy-done.2, f32[256,48,128]{2,0,1:T(8,128)} %copy-done, f32[256,2,128]{2,0,1:T(8,128)S(1)} %collective-permute-done, f32[256,52,2]{2,0,1:T(8,128)} %copy.17), kind=kLoop, calls=%fused_computation.37 | loop fusion | flops 29884416 | bytes 10174464 | tf_op jit(solution)/shard_map/stack | solution.py:41
  95.8 1.7 copy-done.1
  97.4 2.5 fusion.20
  100.0 5.9 %fusion.8 = bf16[255,2,48,128]{3,0,2,1:T(8,128)(2,1)} fusion(bf16[256,1,48,128]{3,0,2,1:T(8,128)(2,1)S(1)} %fusion.17, bf16[256,1,48,128]{3,0,2,1:T(8,128)(2,1)} %copy-done.1), kind=kLoop, calls=%fused_computation.17 | loop fusion | flops 3133440 | bytes 12558336 | tf_op jit(solution)/shard_map/stack | solution.py:41
  105.8 8.7 %copy.22 = bf16[255,2,48,128]{0,3,2,1:T(8,128)(2,1)} copy(bf16[255,2,48,128]{3,0,2,1:T(8,128)(2,1)} %fusion.8) | data formatting | bytes 12533760 | tf_op jit(solution)/shard_map/slice | solution.py:63
  114.5 240.5 %all-reduce.4.cloned.1.call-done = f32[256,256]{0,1:T(8,128)} async-done(((f32[256,256]{0,1:T(8,128)}), f32[256,256]{0,1:T(8,128)}) %all-reduce.4.cloned.1.call-update) | async-done | bytes 262160 | tf_op jit(solution)/shard_map/psum | solution.py:57
  357.1 11.7 %cholesky.51 = f32[128,128]{1,0:T(8,128)S(1)} custom-call(f32[128,128]{1,0:T(8,128)S(1)} %cholesky.124), custom_call_target="Cholesky" | custom-call | tf_op jit(solution)/shard_map/jit(cholesky)/cholesky | solution.py:58
  368.9 9.8 %custom-call.14 = f32[1,128,128]{1,2,0:T(8,128)S(1)} custom-call(f32[1,128,128]{2,1,0:T(8,128)S(1)} %get-tuple-element.50), custom_call_target="InvertDiagBlocksLowerTriangular" | custom-call | tf_op jit(solution)/shard_map/jit(cholesky)/cholesky | solution.py:58
  379.2 11.6 %cholesky.110 = f32[127,127]{1,0:T(8,128)S(1)} custom-call(f32[127,127]{1,0:T(8,128)S(1)} %convolution_subtract_fusion.2), custom_call_target="Cholesky" | custom-call | tf_op jit(solution)/shard_map/jit(cholesky)/cholesky | solution.py:58
  393.6 19.9 %custom-call.17 = f32[2,128,128]{1,2,0:T(8,128)S(1)} custom-call(f32[2,128,128]{2,1,0:T(8,128)S(1)} %pad_maximum_fusion.15), custom_call_target="InvertDiagBlocksLowerTriangular" | custom-call | tf_op jit(solution)/shard_map/triangular_solve/custom-call.0 | solution.py:25
  419.2 4.6 %convolution_convert_fusion = bf16[255,12288]{1,0:T(8,128)(2,1)S(1)} fusion(bf16[255,12288]{0,1:T(8,128)(2,1)} %bitcast.61, bf16[127,255]{1,0:T(8,128)(2,1)S(1)} %fusion.35, f32[128,255]{1,0:T(8,128)S(1)} %fusion.28), kind=kOutput, calls=%fused_computation | convolution fusion | flops 1601447936 | bytes 12729090 | tf_op jit(solution)/shard_map/dot_general | solution.py:63
  425.3 3.8 slice.212
  (45 shorter events, 15.3 us)
Async XLA Ops:
  7.2 347.8 %all-reduce.4.cloned.1.call-start = ((), (), s32[]{:S(2)}) async-start(), calls=%async_computation | async-start | bytes 524288 | tf_op jit(solution)/shard_map/psum | solution.py:57
  12.5 6.9 %copy-start = (f32[256,48,128]{2,0,1:T(8,128)}, f32[256,48,128]{2,0,1:T(8,128)S(1)}, u32[]{:S(2)}) copy-start(f32[256,48,128]{2,0,1:T(8,128)S(1)} %divide_bitcast_fusion) | copy-start | bytes 18874372
  12.5 3.8 collective-permute-start
  14.3 5.1 %collective-permute-start.1 = (f32[256,2,128]{2,0,1:T(8,128)S(1)}, f32[256,2,128]{2,0,1:T(8,128)S(1)}, u32[]{:S(2)}, u32[]{:S(2)}) collective-permute-start(f32[256,2,128]{2,0,1:T(8,128)S(1)} %get-tuple-element.44), channel_id=1, source_target_pairs={{16,0},{32,16},{48,32},{64,48},{80,64},{96,80},{112,96},{128,112},... | collective-permute-start | bytes 786440 | tf_op jit(solution)/shard_map/ppermute | solution.py:17
  19.4 0.7 copy-start.2
  40.1 24.5 %collective-permute-start.2 = (f32[256,52,2]{0,2,1:T(2,128)S(1)}, f32[256,52,2]{0,2,1:T(2,128)}, u32[]{:S(2)}, u32[]{:S(2)}) collective-permute-start(f32[256,52,2]{0,2,1:T(2,128)S(1)} %copy.16), channel_id=1, source_target_pairs={{0,1},{1,2},{2,3},{3,4},{4,5},{5,6},{6,7},{7,8},{8,9},{9,10},{10,1... | collective-permute-start | bytes 319496 | tf_op jit(solution)/shard_map/ppermute | solution.py:15
  48.9 20.7 %collective-permute-start.3 = (f32[256,52,2]{0,2,1:T(2,128)}, f32[256,52,2]{0,2,1:T(2,128)}, u32[]{:S(2)}, u32[]{:S(2)}) collective-permute-start(f32[256,52,2]{0,2,1:T(2,128)} %copy.18), channel_id=1, source_target_pairs={{1,0},{2,1},{3,2},{4,3},{5,4},{6,5},{7,6},{8,7},{9,8},{10,9},{11,1... | collective-permute-start | bytes 319496 | tf_op jit(solution)/shard_map/ppermute | solution.py:17
  95.8 1.7 copy-start.1
  105.8 287.6 %copy-start.4 = (f32[128,1]{1,0:T(8,128)S(1)}, f32[128,1]{1,0:T(8,128)}, u32[]{:S(2)}) copy-start(f32[128,1]{1,0:T(8,128)} %constant.87.clone.3) | copy-start | bytes 1540
  114.5 303.8 %copy-start.3 = (f32[255,255]{1,0:T(8,128)S(1)}, f32[255,255]{1,0:T(8,128)}, u32[]{:S(2)}) copy-start(f32[255,255]{1,0:T(8,128)} %fusion.22) | copy-start | bytes 780304
Sparse Core Ops, SparseCore 0:
  100.1 254.8 all-reduce.3
where the time goes:
time: 437 us; the launch traced here: 436 us
  waiting for transfers between devices  244 us (56%)
  other arithmetic  99.2 us (23%)
  local copies, waits for them, and re-layouts  53.9 us (12%)
  between operations  15.6 us (4%)
  matrix products  12.3 us (3%)
  starting transfers between devices  11.2 us (3%)
    psum x1, waiting for transfers between devices, shards(): gram = lax.psum(local_gram, ('gx', 'gy'))  240 us
    another operation x3, other arithmetic, gradients(): return jnp.stack([grad_x, grad_y], axis=1).astype(jnp.bfloat16)  38 us
    another operation x7, other arithmetic, shards(): lower = jnp.linalg.cholesky(gram[:snaps - 1, :snaps - 1])  34.5 us
    another operation x4, other arithmetic, tri_solve(): return lax.linalg.triangular_solve(lower, right, left_side=True, lower=True)  20.1 us
    slice x3, local copies, waits for them, and re-layouts, padded_2(): lax.slice_in_dim(cells, cells.shape[dim] - width, cells.shape[dim], axis=...  16.4 us
  transfers between devices with their start and end apart: 5, of which 2 were waited for; matrix products, arithmetic and copies ran while one was open for 8% of the time, Pallas kernels for 0%

commit v1 on v0

--- a/solution.py
+++ b/solution.py
@@ -54,7 +54,7 @@
         lax.dot_general(snap, snap, (((1,), (1,)), ((), ())), preferred_element_type=jnp.float32)
         / total_rows
     )
-    gram = lax.psum(local_gram, ("gx", "gy"))
+    gram = lax.psum(lax.psum(local_gram, "gx"), "gy")
     lower = jnp.linalg.cholesky(gram[: snaps - 1, : snaps - 1])
     cross = gram[: snaps - 1, 1:]
     half = tri_solve(lower, cross)

time: 437 us -> 393 us (0.90)
  waiting for transfers between devices: 244 us -> 200 us
    psum x1 -> x2, waiting for transfers between devices: 240 us -> 196 us  [shards(): gram = lax.psum(lax.psum(local_gram, 'gx'), 'gy')]
  transfers between devices with their start and end apart: 5 -> 6, of which waited for: 2 -> 3; matrix products, arithmetic and copies ran while one was open for 8% -> 9% of each run, Pallas kernels for 0% -> 0%
where the time goes in v1:
time: 393 us; the launch traced here: 392 us
  waiting for transfers between devices  200 us (51%)
  other arithmetic  98.8 us (25%)
  local copies, waits for them, and re-layouts  53.9 us (14%)
  between operations  15.6 us (4%)
  matrix products  12.3 us (3%)
  starting transfers between devices  11.5 us (3%)
    psum x2, waiting for transfers between devices, shards(): gram = lax.psum(lax.psum(local_gram, 'gx'), 'gy')  196 us
    another operation x3, other arithmetic, gradients(): return jnp.stack([grad_x, grad_y], axis=1).astype(jnp.bfloat16)  38.2 us
    another operation x7, other arithmetic, shards(): lower = jnp.linalg.cholesky(gram[:snaps - 1, :snaps - 1])  34.5 us
    another operation x4, other arithmetic, tri_solve(): return lax.linalg.triangular_solve(lower, right, left_side=True, lower=True)  20.1 us
    slice x3, local copies, waits for them, and re-layouts, padded_2(): lax.slice_in_dim(cells, cells.shape[dim] - width, cells.shape[dim], axis=...  16.4 us
    slice x1, local copies, waits for them, and re-layouts, shards(): snap[1:]  8.66 us
    unnamed x11, local copies, waits for them, and re-layouts  8.44 us
  transfers between devices with their start and end apart: 6, of which 3 were waited for; matrix products, arithmetic and copies ran while one was open for 9% of the time, Pallas kernels for 0%

profile of v1, /device:TPU:2, one launch (start us, length us, event | category | flops | bytes accessed | tf_op | source)
XLA Modules:
  0.0 392.2 jit_solution(2626920046506720822)
XLA Ops:
  7.2 3.9 %fusion.43 = (bf16[1,256,48,128]{3,2,1,0:T(8,128)(2,1)S(1)}, bf16[1,256,48,128]{3,2,1,0:T(8,128)(2,1)S(1)}) fusion(bf16[2,256,48,128]{3,2,1,0:T(8,128)(2,1)} %param.3), kind=kLoop, calls=%fused_computation.89 | loop fusion | bytes 12582912 | tf_op jit(solution)/shard_map/slice | solution.py:49
  12.5 1.8 collective-permute-start
  15.6 3.8 collective-permute-done.1
  20.1 3.6 pad_maximum_fusion.1
  23.7 11.6 %fusion.41 = (f32[256,52,2]{2,0,1:T(8,128)}, f32[256,52,2]{2,0,1:T(8,128)}) fusion(f32[256,52,128]{2,0,1:T(8,128)} %pad_maximum_fusion.1), kind=kLoop, calls=%fused_computation.87 | loop fusion | bytes 425984 | tf_op jit(solution)/shard_map/slice | solution.py:12
  35.4 4.7 %copy.16 = f32[256,52,2]{0,2,1:T(2,128)S(1)} copy(f32[256,52,2]{2,0,1:T(8,128)} %get-tuple-element.41) | data formatting | bytes 212992 | tf_op jit(solution)/shard_map/slice | solution.py:12
  40.1 3.5 collective-permute-start.2
  43.6 5.3 %copy.18 = f32[256,52,2]{0,2,1:T(2,128)} copy(f32[256,52,2]{2,0,1:T(8,128)} %get-tuple-element.42) | data formatting | bytes 212992 | tf_op jit(solution)/shard_map/slice | solution.py:11
  48.9 4.6 %collective-permute-start.3 = (f32[256,52,2]{0,2,1:T(2,128)}, f32[256,52,2]{0,2,1:T(2,128)}, u32[]{:S(2)}, u32[]{:S(2)}) collective-permute-start(f32[256,52,2]{0,2,1:T(2,128)} %copy.18), channel_id=1, source_target_pairs={{1,0},{2,1},{3,2},{4,3},{5,4},{6,5},{7,6},{8,7},{9,8},{10,9},{11,1... | collective-permute-start | bytes 319496 | tf_op jit(solution)/shard_map/ppermute | solution.py:17
  53.5 11.1 %fusion.17 = bf16[256,1,48,128]{3,0,2,1:T(8,128)(2,1)S(1)} fusion(f32[256,2,128]{2,0,1:T(8,128)} %copy-done.2, f32[256,48,128]{2,0,1:T(8,128)} %copy-done, f32[256,2,128]{2,0,1:T(8,128)S(1)} %collective-permute-done), kind=kLoop, calls=%fused_computation.36 | loop fusion | flops 17301504 | bytes 9961472 | tf_op jit(solution)/shard_map/stack | solution.py:41
  64.6 5.0 %copy.17 = f32[256,52,2]{2,0,1:T(8,128)} copy(f32[256,52,2]{0,2,1:T(2,128)} %collective-permute-done.2) | data formatting | bytes 212992 | tf_op jit(solution)/shard_map/ppermute | solution.py:15
  69.6 5.1 %copy.19 = f32[256,52,2]{2,0,1:T(8,128)} copy(f32[256,52,2]{0,2,1:T(2,128)} %collective-permute-done.3) | data formatting | bytes 212992 | tf_op jit(solution)/shard_map/ppermute | solution.py:17
  74.7 21.3 %fusion.18 = bf16[256,1,48,128]{3,0,2,1:T(8,128)(2,1)S(1)} fusion(f32[256,52,2]{2,0,1:T(8,128)} %copy.19, f32[256,2,128]{2,0,1:T(8,128)} %copy-done.2, f32[256,48,128]{2,0,1:T(8,128)} %copy-done, f32[256,2,128]{2,0,1:T(8,128)S(1)} %collective-permute-done, f32[256,52,2]{2,0,1:T(8,128)} %copy.17), kind=kLoop, calls=%fused_computation.37 | loop fusion | flops 29884416 | bytes 10174464 | tf_op jit(solution)/shard_map/stack | solution.py:41
  97.6 2.5 fusion.20
  100.5 113.0 %all-reduce.5.cloned.1.call-done = f32[256,256]{0,1:T(8,128)} async-done(((f32[256,256]{0,1:T(8,128)}), f32[256,256]{0,1:T(8,128)}) %all-reduce.5.cloned.1.call-update) | async-done | bytes 262160 | tf_op jit(solution)/shard_map/psum | solution.py:57
  213.5 5.9 %fusion.8 = bf16[255,2,48,128]{3,0,2,1:T(8,128)(2,1)} fusion(bf16[256,1,48,128]{3,0,2,1:T(8,128)(2,1)S(1)} %fusion.17, bf16[256,1,48,128]{3,0,2,1:T(8,128)(2,1)} %copy-done.1), kind=kLoop, calls=%fused_computation.17 | loop fusion | flops 3133440 | bytes 12558336 | tf_op jit(solution)/shard_map/stack | solution.py:41
  219.4 8.7 %copy.22 = bf16[255,2,48,128]{0,3,2,1:T(8,128)(2,1)} copy(bf16[255,2,48,128]{3,0,2,1:T(8,128)(2,1)} %fusion.8) | data formatting | bytes 12533760 | tf_op jit(solution)/shard_map/slice | solution.py:63
  228.0 83.3 %all-reduce.7.cloned.1.call-done = f32[256,256]{0,1:T(8,128)} async-done(((f32[256,256]{0,1:T(8,128)}), f32[256,256]{0,1:T(8,128)}) %all-reduce.7.cloned.1.call-update) | async-done | bytes 262160 | tf_op jit(solution)/shard_map/psum | solution.py:57
  313.4 11.7 %cholesky.51 = f32[128,128]{1,0:T(8,128)S(1)} custom-call(f32[128,128]{1,0:T(8,128)S(1)} %cholesky.124), custom_call_target="Cholesky" | custom-call | tf_op jit(solution)/shard_map/jit(cholesky)/cholesky | solution.py:58
  325.2 9.8 %custom-call.14 = f32[1,128,128]{1,2,0:T(8,128)S(1)} custom-call(f32[1,128,128]{2,1,0:T(8,128)S(1)} %get-tuple-element.50), custom_call_target="InvertDiagBlocksLowerTriangular" | custom-call | tf_op jit(solution)/shard_map/jit(cholesky)/cholesky | solution.py:58
  335.5 11.6 %cholesky.110 = f32[127,127]{1,0:T(8,128)S(1)} custom-call(f32[127,127]{1,0:T(8,128)S(1)} %convolution_subtract_fusion.3), custom_call_target="Cholesky" | custom-call | tf_op jit(solution)/shard_map/jit(cholesky)/cholesky | solution.py:58
  349.9 19.9 %custom-call.17 = f32[2,128,128]{1,2,0:T(8,128)S(1)} custom-call(f32[2,128,128]{2,1,0:T(8,128)S(1)} %pad_maximum_fusion.15), custom_call_target="InvertDiagBlocksLowerTriangular" | custom-call | tf_op jit(solution)/shard_map/triangular_solve/custom-call.0 | solution.py:25
  375.5 4.6 %convolution_convert_fusion = bf16[255,12288]{1,0:T(8,128)(2,1)S(1)} fusion(bf16[255,12288]{0,1:T(8,128)(2,1)} %bitcast.62, bf16[127,255]{1,0:T(8,128)(2,1)S(1)} %fusion.35, f32[128,255]{1,0:T(8,128)S(1)} %fusion.27), kind=kOutput, calls=%fused_computation | convolution fusion | flops 1601447936 | bytes 12729090 | tf_op jit(solution)/shard_map/dot_general | solution.py:63
  381.6 3.8 slice.212
  (46 shorter events, 16.5 us)
Async XLA Ops:
  7.2 206.3 %all-reduce.5.cloned.1.call-start = ((), (), s32[]{:S(2)}) async-start(), calls=%async_computation | async-start | bytes 524288 | tf_op jit(solution)/shard_map/psum | solution.py:57
  12.5 6.9 %copy-start = (f32[256,48,128]{2,0,1:T(8,128)}, f32[256,48,128]{2,0,1:T(8,128)S(1)}, u32[]{:S(2)}) copy-start(f32[256,48,128]{2,0,1:T(8,128)S(1)} %divide_bitcast_fusion) | copy-start | bytes 18874372
  12.5 3.1 collective-permute-start
  14.3 5.1 %collective-permute-start.1 = (f32[256,2,128]{2,0,1:T(8,128)S(1)}, f32[256,2,128]{2,0,1:T(8,128)S(1)}, u32[]{:S(2)}, u32[]{:S(2)}) collective-permute-start(f32[256,2,128]{2,0,1:T(8,128)S(1)} %get-tuple-element.44), channel_id=1, source_target_pairs={{16,0},{32,16},{48,32},{64,48},{80,64},{96,80},{112,96},{128,112},... | collective-permute-start | bytes 786440 | tf_op jit(solution)/shard_map/ppermute | solution.py:17
  19.4 0.7 copy-start.2
  40.1 24.5 %collective-permute-start.2 = (f32[256,52,2]{0,2,1:T(2,128)S(1)}, f32[256,52,2]{0,2,1:T(2,128)}, u32[]{:S(2)}, u32[]{:S(2)}) collective-permute-start(f32[256,52,2]{0,2,1:T(2,128)S(1)} %copy.16), channel_id=1, source_target_pairs={{0,1},{1,2},{2,3},{3,4},{4,5},{5,6},{6,7},{7,8},{8,9},{9,10},{10,1... | collective-permute-start | bytes 319496 | tf_op jit(solution)/shard_map/ppermute | solution.py:15
  48.9 20.7 %collective-permute-start.3 = (f32[256,52,2]{0,2,1:T(2,128)}, f32[256,52,2]{0,2,1:T(2,128)}, u32[]{:S(2)}, u32[]{:S(2)}) collective-permute-start(f32[256,52,2]{0,2,1:T(2,128)} %copy.18), channel_id=1, source_target_pairs={{1,0},{2,1},{3,2},{4,3},{5,4},{6,5},{7,6},{8,7},{9,8},{10,9},{11,1... | collective-permute-start | bytes 319496 | tf_op jit(solution)/shard_map/ppermute | solution.py:17
  96.0 1.7 copy-start.1
  100.2 211.2 %all-reduce.7.cloned.1.call-start = ((), (), s32[]{:S(2)}) async-start(), calls=%async_computation.1 | async-start | bytes 524288 | tf_op jit(solution)/shard_map/psum | solution.py:57
  219.4 130.4 %copy-start.3 = (f32[128,1]{1,0:T(8,128)S(1)}, f32[128,1]{1,0:T(8,128)}, u32[]{:S(2)}) copy-start(f32[128,1]{1,0:T(8,128)} %constant.87.clone.3) | copy-start | bytes 1540
Sparse Core Ops, SparseCore 0:
  100.3 113.1 all-reduce.4
  217.0 94.3 all-reduce.6
